TPU v7x, 32 devices: a whole 2x2x4 slice. The times are simulated.
32 devices in a mesh: groups: 2 (over x), rows: 16 (over z, y, core).
Axes of the slice: x: 2, y: 2, z: 4, core: 2. Of those that a mesh axis runs over, the one named last changes fastest.
Arguments:
- student: float32 [8192, 512], P(('groups', 'rows')), parts along dimension 0, may hold values from -6 to 6
- teacher: float32 [8192, 6144], P(('groups', 'rows')), parts along dimension 0, may hold values from -6 to 6
- heads: bfloat16 [512, 6144], P(None, 'rows'), may hold values from -0.25 to 0.25
Outputs:
- grad_student: float32 [8192, 512], P(('groups', 'rows')), parts along dimension 0
- grad_heads: float32 [1024, 6144], P('groups', 'rows'), parts along dimension 0
There are 2 independent parts, one for each index of `groups`. A program takes and returns all parts, laid end to end along the dimension named above; an argument that names none is the same for every part. Nothing has to cross between parts.
All inputs are finite; a program needn't handle non-finite values.
Results may differ from a plain program's by a relative error of at most 0.0026.
Values may be sent and summed in bfloat16 or wider, within the bound.
No kernel may reach another device: no remote copies, remote signals or barrier semaphores. Data moves between devices by JAX's collectives and lax.ppermute only.
A program may use at most 128 MiB of HBM per device.

v0:
```python
import jax
import jax.numpy as jnp
from jax import lax
from jax.sharding import PartitionSpec as P

reg_weight = 0.0625
head_scale = 0.015625


def contract(left, right, left_dim, right_dim):
    return lax.dot_general(
        left,
        right,
        (((left_dim,), (right_dim,)), ((), ())),
        precision=lax.Precision.HIGHEST,
        preferred_element_type=jnp.float32,
    )


def per_device(student, teacher, heads):
    devices = lax.axis_size("rows")
    rows_here, model_width = student.shape
    total_rows = rows_here * devices
    positions = jnp.arange(model_width)
    weights = (
        1.0
        + (positions < model_width // 4).astype(jnp.float32)
        + (positions < model_width // 2).astype(jnp.float32)
    )
    nested = jnp.minimum(weights[:, None], weights[None, :])
    gram_scale = 0.5 / total_rows
    wide_here = heads.astype(jnp.float32)
    moment = lax.psum(contract(student, student, 0, 0), "rows")
    cross_here = lax.psum_scatter(
        contract(teacher, student, 0, 0), "rows", scatter_dimension=0, tiled=True
    )
    grad_heads = head_scale * (contract(moment, wide_here, 1, 0) - cross_here.T)
    cross_sent = cross_here.T.astype(jnp.bfloat16)
    gathered = (
        lax.all_gather(heads, "rows", axis=1, tiled=True),
        lax.all_gather(cross_sent, "rows", axis=1, tiled=True),
    )
    wide_all = gathered[0].astype(jnp.float32)
    cross_all = gathered[1].astype(jnp.float32)
    error = contract(student, wide_all, 1, 0) - teacher
    shared = (
        reg_weight * contract(error, wide_all, 1, 1)
        - gram_scale * contract(teacher, cross_all, 1, 1) * weights[None, :]
    )
    grad_student = shared + gram_scale * contract(student, moment * nested, 1, 0)
    return (grad_student, grad_heads)


def solution(mesh):
    in_specs = (P(("groups", "rows"), None), P(("groups", "rows"), None), P(None, "rows"))
    out_specs = (P(("groups", "rows"), None), P("groups", "rows"))
    return jax.shard_map(
        per_device, mesh=mesh, in_specs=in_specs, out_specs=out_specs, check_vma=False
    )
```

profile of v0, /device:TPU:0, one launch (start us, length us, event | category | flops | bytes accessed | tf_op | source)
XLA Modules:
  0.0 414.8 jit_solution(12258084241356141119)
XLA Ops:
  7.2 0.0 copy-start
  7.2 0.0 reduce-scatter.2.cloned.1.call-start
  7.2 1.0 copy-done
  8.2 14.8 %fusion.9 = f32[6144,512]{1,0:T(8,128)} fusion(f32[256,6144]{1,0:T(8,128)} %param.4, f32[256,512]{1,0:T(8,128)S(1)} %copy-done), kind=kOutput, calls=%fused_computation.19 | convolution fusion | flops 9663676416 | bytes 19398656 | tf_op jit(solution)/shard_map/dot_general | solution.py:11
  23.0 0.0 reduce-scatter.2.cloned.1.call-update
  23.0 0.0 all-gather.3.cloned.1.call-start
  23.0 0.7 all-gather.3.cloned.1.call-update
  23.8 0.0 all-reduce.2.cloned.1.call-start
  23.8 2.0 fusion.10
  25.8 0.0 all-reduce.2.cloned.1.call-update
  25.9 0.2 all-gather.5.cloned.1.call-start
  26.1 134.4 %reduce-scatter.2.cloned.1.call-done = f32[384,512]{1,0:T(8,128)} async-done(((f32[6144,512]{1,0:T(8,128)}), f32[384,512]{1,0:T(8,128)}) %reduce-scatter.2.cloned.1.call-update) | async-done | bytes 786448 | tf_op jit(solution)/shard_map/reduce_scatter | solution.py:34
  160.5 1.9 bitcast_convert_fusion
  162.4 0.0 all-gather.5.cloned.1.call-update
  162.4 0.0 copy-start.2
  162.5 0.0 copy-start.3
  162.5 65.0 %all-gather.3.cloned.1.call-done = bf16[512,6144]{1,0:T(8,128)(2,1)} async-done(((bf16[512,384]{1,0:T(8,128)(2,1)}), bf16[512,6144]{1,0:T(8,128)(2,1)}) %all-gather.3.cloned.1.call-update) | async-done | bytes 6291472 | tf_op jit(solution)/shard_map/all_gather | solution.py:40
  227.5 10.7 %convolution_subtract_fusion = f32[256,6144]{1,0:T(8,128)} fusion(f32[256,6144]{1,0:T(8,128)} %param.4, f32[256,512]{1,0:T(8,128)S(1)} %copy-done, bf16[512,6144]{1,0:T(8,128)(2,1)} %all-gather.3.cloned.1.call-done), kind=kOutput, calls=%fused_computation | convolution fusion | flops 9665249280 | bytes 19398656 | tf_op jit(solution)/shard_map/dot_general | solution.py:11
  238.2 84.2 %all-reduce.2.cloned.1.call-done = f32[512,512]{1,0:T(8,128)} async-done(((f32[512,512]{1,0:T(8,128)}), f32[512,512]{1,0:T(8,128)}) %all-reduce.2.cloned.1.call-update) | async-done | bytes 1048592 | tf_op jit(solution)/shard_map/psum | solution.py:33
  322.4 0.0 copy-done.2
  322.4 0.0 copy-done.3
  322.4 2.1 fusion
  324.5 1.1 copy.8
  325.7 60.6 %all-gather.5.cloned.1.call-done = bf16[512,6144]{0,1:T(8,128)(2,1)} async-done(((bf16[512,384]{0,1:T(8,128)(2,1)}), bf16[512,6144]{0,1:T(8,128)(2,1)}) %all-gather.5.cloned.1.call-update) | async-done | bytes 6291472 | tf_op jit(solution)/shard_map/all_gather | solution.py:41
  386.3 9.8 %fusion.3 = f32[256,512]{1,0:T(8,128)S(1)} fusion(bf16[512,6144]{0,1:T(8,128)(2,1)} %all-gather.5.cloned.1.call-done, f32[256,6144]{1,0:T(8,128)} %param.4, f32[512]{0:T(512)S(1)} %broadcast_multiply_fusion), kind=kOutput, calls=%fused_computation.7 | convolution fusion | flops 9663807488 | bytes 13109248 | tf_op jit(solution)/shard_map/dot_general | solution.py:11
  396.1 0.0 copy-start.1
  396.1 10.1 %fusion.4 = f32[256,512]{1,0:T(8,128)S(1)} fusion(f32[256,512]{1,0:T(8,128)S(1)} %fusion.3, f32[256,6144]{1,0:T(8,128)} %convolution_subtract_fusion, bf16[512,6144]{1,0:T(8,128)(2,1)} %all-gather.3.cloned.1.call-done), kind=kOutput, calls=%fused_computation.9 | convolution fusion | flops 9663938560 | bytes 13631488 | tf_op jit(solution)/shard_map/dot_general | solution.py:11
  406.2 0.0 copy-done.1
  406.2 2.1 fusion.2
  (2 shorter events, 0.0 us)
Async XLA Ops:
  7.2 1.0 copy-start
  7.2 153.3 %reduce-scatter.2.cloned.1.call-start = ((), (), s32[]{:S(2)}) async-start(), calls=%async_computation.2 | async-start | bytes 13369344 | tf_op jit(solution)/shard_map/reduce_scatter | solution.py:34
  23.0 204.5 %all-gather.3.cloned.1.call-start = ((), (), s32[]{:S(2)}) async-start(), calls=%async_computation.1 | async-start | bytes 6684672 | tf_op jit(solution)/shard_map/all_gather | solution.py:40
  23.8 298.7 %all-reduce.2.cloned.1.call-start = ((), (), s32[]{:S(2)}) async-start(), calls=%async_computation.4 | async-start | bytes 2097152 | tf_op jit(solution)/shard_map/psum | solution.py:33
  25.9 360.4 %all-gather.5.cloned.1.call-start = ((), (), s32[]{:S(2)}) async-start(), calls=%async_computation.3 | async-start | bytes 6684672 | tf_op jit(solution)/shard_map/all_gather | solution.py:41
  162.4 160.0 %copy-start.2 = (f32[384,512]{1,0:T(8,128)S(1)}, f32[384,512]{1,0:T(8,128)}, u32[]{:S(2)}) copy-start(f32[384,512]{1,0:T(8,128)} %reduce-scatter.2.cloned.1.call-done) | copy-start | bytes 2359300
  162.5 160.0 %copy-start.3 = (bf16[512,384]{1,0:T(8,128)(2,1)S(1)}, bf16[512,384]{1,0:T(8,128)(2,1)}, u32[]{:S(2)}) copy-start(bf16[512,384]{1,0:T(8,128)(2,1)} %param.5) | copy-start | bytes 1179652
  396.1 10.1 %copy-start.1 = (f32[512,512]{1,0:T(8,128)S(1)}, f32[512,512]{1,0:T(8,128)}, u32[]{:S(2)}) copy-start(f32[512,512]{1,0:T(8,128)} %all-reduce.2.cloned.1.call-done) | copy-start | bytes 3145732
Sparse Core Ops, SparseCore 0:
  23.1 137.3 reduce-scatter.1
  162.6 64.7 all-gather.2
  230.9 91.4 all-reduce.1
  325.1 61.0 all-gather.4
where the time goes:
time: 415 us
  waiting for transfers between devices  345 us (83%)
  matrix products  51.6 us (12%)
  between operations  13.8 us (3%)
    reduce_scatter x1, waiting for transfers between devices, per_device(): lax.psum_scatter(contract(teacher, student, 0, 0), 'rows', scatter_dimens...  134 us
    psum x1, waiting for transfers between devices, per_device(): moment = lax.psum(contract(student, student, 0, 0), 'rows')  84.2 us
    all_gather x1, waiting for transfers between devices, per_device(): lax.all_gather(heads, 'rows', axis=1, tiled=True)  65 us
    all_gather x1, waiting for transfers between devices, per_device(): lax.all_gather(cross_sent, 'rows', axis=1, tiled=True)  60.6 us
    dot_general x7, matrix products, contract(): lax.dot_general(left, right, (((left_dim,), (right_dim,)), ((), ())), pre...  51.6 us
  transfers between devices with their start and end apart: 4, of which 4 were waited for; matrix products, arithmetic and copies ran while one was open for 4% of the time, Pallas kernels for 0%

commit v1 on v0

--- a/solution.py
+++ b/solution.py
@@ -36,10 +36,28 @@
     )
     grad_heads = head_scale * (contract(moment, wide_here, 1, 0) - cross_here.T)
     cross_sent = cross_here.T.astype(jnp.bfloat16)
-    gathered = (
-        lax.all_gather(heads, "rows", axis=1, tiled=True),
-        lax.all_gather(cross_sent, "rows", axis=1, tiled=True),
-    )
+
+    def measure_the_results(inp):
+        placed = lax.axis_size("rows")
+        o_now = lax.axis_index("rows")
+        aux, odd, x_new = (placed, o_now, inp.shape[1])
+        copies = [(d, (d + 1) % aux) for d in range(aux)]
+        found = [(d, (d - 1) % aux) for d in range(aux)]
+        top = jnp.zeros((*inp.shape[:1], aux * x_new, *inp.shape[2:]), inp.dtype)
+        top = lax.dynamic_update_slice_in_dim(top, inp, odd * x_new, axis=1)
+        reply = part_now = inp
+        piece_next = aux // 2
+        for t in range(1, piece_next + 1):
+            reply = lax.ppermute(reply, "rows", copies)
+            top = lax.dynamic_update_slice_in_dim(top, reply, (odd - t) % aux * x_new, axis=1)
+            if t < aux - piece_next:
+                part_now = lax.ppermute(part_now, "rows", found)
+                top = lax.dynamic_update_slice_in_dim(
+                    top, part_now, (odd + t) % aux * x_new, axis=1
+                )
+        return top
+
+    gathered = (lax.all_gather(heads, "rows", axis=1, tiled=True), measure_the_results(cross_sent))
     wide_all = gathered[0].astype(jnp.float32)
     cross_all = gathered[1].astype(jnp.float32)
     error = contract(student, wide_all, 1, 0) - teacher

time: 415 us -> 395 us (0.952)
  waiting for transfers between devices: 345 us -> 273 us
  starting transfers between devices: 0.34 us -> 32.7 us
  local copies, waits for them, and re-layouts: 2.16 us -> 27.2 us
  matrix products: 51.6 us -> 46.4 us
    all_gather x1 -> x0, waiting for transfers between devices: 60.6 us -> none  [per_device(): lax.all_gather(cross_sent, 'rows', axis=1, tiled=True)]
    ppermute x0 -> x15, starting transfers between devices: none -> 32.6 us  [the longest x7 22.2 us: measure_the_results(): part_now = lax.ppermute(part_now, 'rows', found)]
    dynamic_update_slice x0 -> x15, local copies, waits for them, and re-layouts: none -> 20.8 us  [the longest x8 11.4 us: measure_the_results(): lax.dynamic_update_slice_in_dim(top, reply, (odd - t) % aux * x_new, axis=1)]
    all_gather x1, waiting for transfers between devices: 65 us -> 46.9 us  [per_device(): lax.all_gather(heads, 'rows', axis=1, tiled=True)]
    ppermute x0 -> x15, waiting for transfers between devices: none -> 15.4 us  [the longest x8 12.5 us: measure_the_results(): reply = lax.ppermute(reply, 'rows', copies)]
    psum x1, waiting for transfers between devices: 84.2 us -> 73.3 us  [per_device(): moment = lax.psum(contract(student, student, 0, 0), 'rows')]
    dot_general x7, matrix products: 51.6 us -> 46.4 us  [contract(): lax.dot_general(left, right, (((left_dim,), (right_dim,)), ((), ())), pre...]
  transfers between devices with their start and end apart: 4 -> 18, of which waited for: 4 -> 9; matrix products, arithmetic and copies ran while one was open for 4% -> 12% of each run, Pallas kernels for 0% -> 0%
where the time goes in v1:
time: 395 us; the launch traced here: 394 us
  waiting for transfers between devices  273 us (69%)
  matrix products  46.4 us (12%)
  starting transfers between devices  32.7 us (8%)
  local copies, waits for them, and re-layouts  27.2 us (7%)
  between operations  14.2 us (4%)
    reduce_scatter x1, waiting for transfers between devices, per_device(): lax.psum_scatter(contract(teacher, student, 0, 0), 'rows', scatter_dimens...  137 us
    psum x1, waiting for transfers between devices, per_device(): moment = lax.psum(contract(student, student, 0, 0), 'rows')  73.3 us
    all_gather x1, waiting for transfers between devices, per_device(): lax.all_gather(heads, 'rows', axis=1, tiled=True)  46.9 us
    dot_general x7, matrix products, contract(): lax.dot_general(left, right, (((left_dim,), (right_dim,)), ((), ())), pre...  46.4 us
    ppermute x7, starting transfers between devices, measure_the_results(): part_now = lax.ppermute(part_now, 'rows', found)  22.2 us
    ppermute x8, waiting for transfers between devices, measure_the_results(): reply = lax.ppermute(reply, 'rows', copies)  12.5 us
    dynamic_update_slice x8, local copies, waits for them, and re-layouts, measure_the_results(): lax.dynamic_update_slice_in_dim(top, reply, (odd - t) % aux * x_new, axis=1)  11.4 us
    ppermute x8, starting transfers between devices, measure_the_results(): reply = lax.ppermute(reply, 'rows', copies)  10.4 us
  transfers between devices with their start and end apart: 18, of which 9 were waited for; matrix products, arithmetic and copies ran while one was open for 12% of the time, Pallas kernels for 0%

profile of v1, /device:TPU:0, one launch (start us, length us, event | category | flops | bytes accessed | tf_op | source)
XLA Modules:
  0.0 394.4 jit_solution(17530857213697517297)
XLA Ops:
  7.2 0.0 copy-start
  7.2 0.0 reduce-scatter.2.cloned.1.call-start
  7.2 1.0 copy-done
  8.2 14.7 %fusion.9 = f32[6144,512]{1,0:T(8,128)} fusion(f32[256,6144]{1,0:T(8,128)} %param.4, f32[256,512]{1,0:T(8,128)S(1)} %copy-done), kind=kOutput, calls=%fused_computation.35 | convolution fusion | flops 9663676416 | bytes 19398656 | tf_op jit(solution)/shard_map/dot_general | solution.py:11
  22.9 0.0 reduce-scatter.2.cloned.1.call-update
  23.0 0.0 all-gather.2.cloned.1.call-start
  23.0 0.7 all-gather.2.cloned.1.call-update
  23.7 0.0 all-reduce.2.cloned.1.call-start
  23.8 136.7 %reduce-scatter.2.cloned.1.call-done = f32[384,512]{1,0:T(8,128)} async-done(((f32[6144,512]{1,0:T(8,128)}), f32[384,512]{1,0:T(8,128)}) %reduce-scatter.2.cloned.1.call-update) | async-done | bytes 786448 | tf_op jit(solution)/shard_map/reduce_scatter | solution.py:34
  160.4 3.0 broadcast_in_dim.2
  163.5 0.8 constant_dynamic-update-slice_fusion.15
  164.3 0.0 collective-permute-start
  164.3 4.4 %collective-permute-start.1 = (bf16[512,384]{0,1:T(8,128)(2,1)S(1)}, bf16[512,384]{0,1:T(8,128)(2,1)S(1)}, u32[]{:S(2)}, u32[]{:S(2)}) collective-permute-start(bf16[512,384]{0,1:T(8,128)(2,1)S(1)} %get-tuple-element.5), channel_id=1, source_target_pairs={{0,15},{1,0},{2,1},{3,2},{4,3},{5,4},{6,5},{7,6},{8,7},{9,8},{10,9... | collective-permute-start | bytes 1179656 | tf_op jit(solution)/shard_map/ppermute | solution.py:54
  168.7 5.6 %collective-permute-done = bf16[512,384]{0,1:T(8,128)(2,1)S(1)} collective-permute-done((bf16[512,384]{0,1:T(8,128)(2,1)S(1)}, bf16[512,384]{0,1:T(8,128)(2,1)S(1)}, u32[]{:S(2)}, u32[]{:S(2)}) %collective-permute-start) | collective-permute-done | bytes 393248 | tf_op jit(solution)/shard_map/ppermute | solution.py:51
  174.4 4.7 %collective-permute-start.2 = (bf16[512,384]{0,1:T(8,128)(2,1)S(1)}, bf16[512,384]{0,1:T(8,128)(2,1)S(1)}, u32[]{:S(2)}, u32[]{:S(2)}) collective-permute-start(bf16[512,384]{0,1:T(8,128)(2,1)S(1)} %collective-permute-done), channel_id=1, source_target_pairs={{0,1},{1,2},{2,3},{3,4},{4,5},{5,6},{6,7},{7,8},{8,9},{9,10},{10,1... | collective-permute-start | bytes 1179656 | tf_op jit(solution)/shard_map/ppermute | solution.py:51
  179.1 2.1 fusion.10
  181.2 0.0 all-reduce.2.cloned.1.call-update
  181.5 0.0 collective-permute-done.1
  181.6 1.4 collective-permute-start.3
  183.0 1.5 collective-permute-done.2
  184.5 5.6 %collective-permute-start.4 = (bf16[512,384]{0,1:T(8,128)(2,1)S(1)}, bf16[512,384]{0,1:T(8,128)(2,1)S(1)}, u32[]{:S(2)}, u32[]{:S(2)}) collective-permute-start(bf16[512,384]{0,1:T(8,128)(2,1)S(1)} %collective-permute-done.2), channel_id=1, source_target_pairs={{0,1},{1,2},{2,3},{3,4},{4,5},{5,6},{6,7},{7,8},{8,9},{9,10},{10,1... | collective-permute-start | bytes 1179656 | tf_op jit(solution)/shard_map/ppermute | solution.py:51
  190.1 46.9 %all-gather.2.cloned.1.call-done = bf16[512,6144]{1,0:T(8,128)(2,1)} async-done(((bf16[512,384]{1,0:T(8,128)(2,1)}), bf16[512,6144]{1,0:T(8,128)(2,1)}) %all-gather.2.cloned.1.call-update) | async-done | bytes 6291472 | tf_op jit(solution)/shard_map/all_gather | solution.py:60
  237.1 10.2 %convolution_subtract_fusion = f32[256,6144]{1,0:T(8,128)S(1)} fusion(f32[256,6144]{1,0:T(8,128)} %param.4, f32[256,512]{1,0:T(8,128)S(1)} %copy-done, bf16[512,6144]{1,0:T(8,128)(2,1)} %all-gather.2.cloned.1.call-done), kind=kOutput, calls=%fused_computation | convolution fusion | flops 9665249280 | bytes 19398656 | tf_op jit(solution)/shard_map/dot_general | solution.py:11
  247.3 0.0 collective-permute-done.3
  247.3 1.6 collective-permute-start.5
  248.9 0.0 collective-permute-done.4
  248.9 0.0 collective-permute-start.6
  248.9 5.9 %convolution_multiply_fusion.2 = f32[256,512]{1,0:T(8,128)} fusion(f32[256,6144]{1,0:T(8,128)S(1)} %convolution_subtract_fusion, bf16[512,6144]{1,0:T(8,128)(2,1)S(1)} %copy-done.1), kind=kOutput, calls=%fused_computation.8 | convolution fusion | flops 9663807488 | bytes 13107200 | tf_op jit(solution)/shard_map/dot_general | solution.py:11
  254.8 0.7 collective-permute-done.5
  255.5 4.7 %collective-permute-start.7 = (bf16[512,384]{0,1:T(8,128)(2,1)}, bf16[512,384]{0,1:T(8,128)(2,1)}, u32[]{:S(2)}, u32[]{:S(2)}) collective-permute-start(bf16[512,384]{0,1:T(8,128)(2,1)} %collective-permute-done.5), channel_id=1, source_target_pairs={{0,15},{1,0},{2,1},{3,2},{4,3},{5,4},{6,5},{7,6},{8,7},{9,8},{10,9... | collective-permute-start | bytes 1179656 | tf_op jit(solution)/shard_map/ppermute | solution.py:54
  260.3 0.7 collective-permute-done.6
  261.0 0.0 collective-permute-start.8
  261.0 73.3 %all-reduce.2.cloned.1.call-done = f32[512,512]{1,0:T(8,128)} async-done(((f32[512,512]{1,0:T(8,128)}), f32[512,512]{1,0:T(8,128)}) %all-reduce.2.cloned.1.call-update) | async-done | bytes 1048592 | tf_op jit(solution)/shard_map/psum | solution.py:33
  334.4 3.3 fusion
  337.7 2.3 copy.8
  339.9 1.8 constant_dynamic-update-slice_fusion.14
  341.8 0.0 collective-permute-done.7
  341.8 1.1 collective-permute-start.9
  342.9 1.8 constant_dynamic-update-slice_fusion.13
  344.7 0.0 collective-permute-done.8
  344.7 0.0 collective-permute-start.10
  344.7 1.8 constant_dynamic-update-slice_fusion.12
  346.4 1.8 constant_dynamic-update-slice_fusion.11
  348.2 1.9 constant_dynamic-update-slice_fusion.10
  350.2 0.0 collective-permute-done.9
  350.2 4.5 %collective-permute-start.11 = (bf16[512,384]{0,1:T(8,128)(2,1)S(1)}, bf16[512,384]{0,1:T(8,128)(2,1)S(1)}, u32[]{:S(2)}, u32[]{:S(2)}) collective-permute-start(bf16[512,384]{0,1:T(8,128)(2,1)S(1)} %collective-permute-done.9), channel_id=1, source_target_pairs={{0,15},{1,0},{2,1},{3,2},{4,3},{5,4},{6,5},{7,6},{8,7},{9,8},{10,9... | collective-permute-start | bytes 1179656 | tf_op jit(solution)/shard_map/ppermute | solution.py:54
  354.6 1.8 constant_dynamic-update-slice_fusion.9
  356.4 0.0 collective-permute-done.10
  356.4 0.0 collective-permute-start.12
  356.4 1.8 constant_dynamic-update-slice_fusion.8
  358.2 1.8 constant_dynamic-update-slice_fusion.7
  360.0 1.8 constant_dynamic-update-slice_fusion.6
  361.7 0.0 collective-permute-done.11
  361.7 4.4 %collective-permute-start.13 = (bf16[512,384]{0,1:T(8,128)(2,1)S(1)}, bf16[512,384]{0,1:T(8,128)(2,1)S(1)}, u32[]{:S(2)}, u32[]{:S(2)}) collective-permute-start(bf16[512,384]{0,1:T(8,128)(2,1)S(1)} %collective-permute-done.11), channel_id=1, source_target_pairs={{0,15},{1,0},{2,1},{3,2},{4,3},{5,4},{6,5},{7,6},{8,7},{9,8},{10,9... | collective-permute-start | bytes 1179656 | tf_op jit(solution)/shard_map/ppermute | solution.py:54
  366.2 0.8 constant_dynamic-update-slice_fusion.5
  367.0 0.8 constant_dynamic-update-slice_fusion.4
  367.8 0.8 constant_dynamic-update-slice_fusion.3
  368.5 0.8 constant_dynamic-update-slice_fusion.2
  369.3 2.2 collective-permute-done.13
  371.5 0.8 constant_dynamic-update-slice_fusion.1
  372.2 4.6 %collective-permute-done.14 = bf16[512,384]{0,1:T(8,128)(2,1)S(1)} collective-permute-done((bf16[512,384]{0,1:T(8,128)(2,1)S(1)}, bf16[512,384]{0,1:T(8,128)(2,1)S(1)}, u32[]{:S(2)}, u32[]{:S(2)}) %collective-permute-start.14) | collective-permute-done | bytes 393248 | tf_op jit(solution)/shard_map/ppermute | solution.py:51
  376.9 0.8 constant_dynamic-update-slice_fusion
  377.7 8.1 %fusion.4 = f32[256,512]{1,0:T(8,128)S(1)} fusion(f32[256,512]{1,0:T(8,128)S(1)} %copy-done.4, bf16[512,6144]{0,1:T(8,128)(2,1)} %constant_dynamic-update-slice_fusion, f32[256,6144]{1,0:T(8,128)S(1)} %bitcast.26, f32[512]{0:T(512)S(1)} %broadcast_multiply_fusion), kind=kOutput, calls=%fused_computation.9 | convolution fusion | flops 9663938560 | bytes 13633536 | tf_op jit(solution)/shard_map/dot_general | solution.py:11
  385.8 2.1 fusion.2
  (27 shorter events, 0.1 us)
Async XLA Ops:
  7.2 1.0 copy-start
  7.2 153.3 %reduce-scatter.2.cloned.1.call-start = ((), (), s32[]{:S(2)}) async-start(), calls=%async_computation.2 | async-start | bytes 13369344 | tf_op jit(solution)/shard_map/reduce_scatter | solution.py:34
  23.0 214.1 %all-gather.2.cloned.1.call-start = ((), (), s32[]{:S(2)}) async-start(), calls=%async_computation.1 | async-start | bytes 6684672 | tf_op jit(solution)/shard_map/all_gather | solution.py:60
  23.7 310.6 %all-reduce.2.cloned.1.call-start = ((), (), s32[]{:S(2)}) async-start(), calls=%async_computation.3 | async-start | bytes 2097152 | tf_op jit(solution)/shard_map/psum | solution.py:33
  160.4 3.0 copy-start.3
  164.3 10.1 %collective-permute-start = (bf16[512,384]{0,1:T(8,128)(2,1)S(1)}, bf16[512,384]{0,1:T(8,128)(2,1)S(1)}, u32[]{:S(2)}, u32[]{:S(2)}) collective-permute-start(bf16[512,384]{0,1:T(8,128)(2,1)S(1)} %get-tuple-element.5), channel_id=1, source_target_pairs={{0,1},{1,2},{2,3},{3,4},{4,5},{5,6},{6,7},{7,8},{8,9},{9,10},{10,1... | collective-permute-start | bytes 1179656 | tf_op jit(solution)/shard_map/ppermute | solution.py:51
  164.3 17.2 %collective-permute-start.1 = (bf16[512,384]{0,1:T(8,128)(2,1)S(1)}, bf16[512,384]{0,1:T(8,128)(2,1)S(1)}, u32[]{:S(2)}, u32[]{:S(2)}) collective-permute-start(bf16[512,384]{0,1:T(8,128)(2,1)S(1)} %get-tuple-element.5), channel_id=1, source_target_pairs={{0,15},{1,0},{2,1},{3,2},{4,3},{5,4},{6,5},{7,6},{8,7},{9,8},{10,9... | collective-permute-start | bytes 1179656 | tf_op jit(solution)/shard_map/ppermute | solution.py:54
  174.3 72.9 %copy-start.7 = (bf16[512,384]{0,1:T(8,128)(2,1)}, bf16[512,384]{0,1:T(8,128)(2,1)S(1)}, u32[]{:S(2)}) copy-start(bf16[512,384]{0,1:T(8,128)(2,1)S(1)} %collective-permute-done) | copy-start | bytes 1179652
  174.4 10.1 %collective-permute-start.2 = (bf16[512,384]{0,1:T(8,128)(2,1)S(1)}, bf16[512,384]{0,1:T(8,128)(2,1)S(1)}, u32[]{:S(2)}, u32[]{:S(2)}) collective-permute-start(bf16[512,384]{0,1:T(8,128)(2,1)S(1)} %collective-permute-done), channel_id=1, source_target_pairs={{0,1},{1,2},{2,3},{3,4},{4,5},{5,6},{6,7},{7,8},{8,9},{9,10},{10,1... | collective-permute-start | bytes 1179656 | tf_op jit(solution)/shard_map/ppermute | solution.py:51
  181.5 65.8 %copy-start.6 = (bf16[512,384]{0,1:T(8,128)(2,1)}, bf16[512,384]{0,1:T(8,128)(2,1)S(1)}, u32[]{:S(2)}) copy-start(bf16[512,384]{0,1:T(8,128)(2,1)S(1)} %collective-permute-done.1) | copy-start | bytes 1179652
  181.6 65.8 %collective-permute-start.3 = (bf16[512,384]{0,1:T(8,128)(2,1)S(1)}, bf16[512,384]{0,1:T(8,128)(2,1)S(1)}, u32[]{:S(2)}, u32[]{:S(2)}) collective-permute-start(bf16[512,384]{0,1:T(8,128)(2,1)S(1)} %collective-permute-done.1), channel_id=1, source_target_pairs={{0,15},{1,0},{2,1},{3,2},{4,3},{5,4},{6,5},{7,6},{8,7},{9,8},{10,9... | collective-permute-start | bytes 1179656 | tf_op jit(solution)/shard_map/ppermute | solution.py:54
  184.5 62.8 %copy-start.5 = (bf16[512,384]{0,1:T(8,128)(2,1)}, bf16[512,384]{0,1:T(8,128)(2,1)S(1)}, u32[]{:S(2)}) copy-start(bf16[512,384]{0,1:T(8,128)(2,1)S(1)} %collective-permute-done.2) | copy-start | bytes 1179652
  184.5 64.4 %collective-permute-start.4 = (bf16[512,384]{0,1:T(8,128)(2,1)S(1)}, bf16[512,384]{0,1:T(8,128)(2,1)S(1)}, u32[]{:S(2)}, u32[]{:S(2)}) collective-permute-start(bf16[512,384]{0,1:T(8,128)(2,1)S(1)} %collective-permute-done.2), channel_id=1, source_target_pairs={{0,1},{1,2},{2,3},{3,4},{4,5},{5,6},{6,7},{7,8},{8,9},{9,10},{10,1... | collective-permute-start | bytes 1179656 | tf_op jit(solution)/shard_map/ppermute | solution.py:51
  237.1 11.9 %copy-start.1 = (bf16[512,6144]{1,0:T(8,128)(2,1)S(1)}, bf16[512,6144]{1,0:T(8,128)(2,1)}, u32[]{:S(2)}) copy-start(bf16[512,6144]{1,0:T(8,128)(2,1)} %all-gather.2.cloned.1.call-done) | copy-start | bytes 18874372
  247.3 7.5 %copy-start.8 = (bf16[512,384]{0,1:T(8,128)(2,1)}, bf16[512,384]{0,1:T(8,128)(2,1)S(1)}, u32[]{:S(2)}) copy-start(bf16[512,384]{0,1:T(8,128)(2,1)S(1)} %collective-permute-done.3) | copy-start | bytes 1179652
  247.3 8.2 %collective-permute-start.5 = (bf16[512,384]{0,1:T(8,128)(2,1)S(1)}, bf16[512,384]{0,1:T(8,128)(2,1)}, u32[]{:S(2)}, u32[]{:S(2)}) collective-permute-start(bf16[512,384]{0,1:T(8,128)(2,1)S(1)} %collective-permute-done.3), channel_id=1, source_target_pairs={{0,15},{1,0},{2,1},{3,2},{4,3},{5,4},{6,5},{7,6},{8,7},{9,8},{10,9... | collective-permute-start | bytes 1179656 | tf_op jit(solution)/shard_map/ppermute | solution.py:54
  248.9 5.9 %copy-start.9 = (bf16[512,384]{0,1:T(8,128)(2,1)}, bf16[512,384]{0,1:T(8,128)(2,1)S(1)}, u32[]{:S(2)}) copy-start(bf16[512,384]{0,1:T(8,128)(2,1)S(1)} %collective-permute-done.4) | copy-start | bytes 1179652
  248.9 12.1 %collective-permute-start.6 = (bf16[512,384]{0,1:T(8,128)(2,1)S(1)}, bf16[512,384]{0,1:T(8,128)(2,1)}, u32[]{:S(2)}, u32[]{:S(2)}) collective-permute-start(bf16[512,384]{0,1:T(8,128)(2,1)S(1)} %collective-permute-done.4), channel_id=1, source_target_pairs={{0,1},{1,2},{2,3},{3,4},{4,5},{5,6},{6,7},{7,8},{8,9},{9,10},{10,1... | collective-permute-start | bytes 1179656 | tf_op jit(solution)/shard_map/ppermute | solution.py:51
  255.5 86.2 %collective-permute-start.7 = (bf16[512,384]{0,1:T(8,128)(2,1)}, bf16[512,384]{0,1:T(8,128)(2,1)}, u32[]{:S(2)}, u32[]{:S(2)}) collective-permute-start(bf16[512,384]{0,1:T(8,128)(2,1)} %collective-permute-done.5), channel_id=1, source_target_pairs={{0,15},{1,0},{2,1},{3,2},{4,3},{5,4},{6,5},{7,6},{8,7},{9,8},{10,9... | collective-permute-start | bytes 1179656 | tf_op jit(solution)/shard_map/ppermute | solution.py:54
  261.0 83.7 %collective-permute-start.8 = (bf16[512,384]{0,1:T(8,128)(2,1)}, bf16[512,384]{0,1:T(8,128)(2,1)}, u32[]{:S(2)}, u32[]{:S(2)}) collective-permute-start(bf16[512,384]{0,1:T(8,128)(2,1)} %collective-permute-done.6), channel_id=1, source_target_pairs={{0,1},{1,2},{2,3},{3,4},{4,5},{5,6},{6,7},{7,8},{8,9},{9,10},{10,1... | collective-permute-start | bytes 1179656 | tf_op jit(solution)/shard_map/ppermute | solution.py:51
  334.4 43.3 %slice-start = ((s8[6291456]{0:T(1024)(128)(4,1)}), s8[2097152]{0:T(1024)(128)(4,1)S(1)}, s32[]{:S(2)}) async-start(s8[6291456]{0:T(1024)(128)(4,1)} %bitcast.25), calls=%async_computation.4 | async-start | bytes 4194304
  339.9 37.7 %copy-start.4 = (f32[256,512]{1,0:T(8,128)S(1)}, f32[256,512]{1,0:T(8,128)}, u32[]{:S(2)}) copy-start(f32[256,512]{1,0:T(8,128)} %convolution_multiply_fusion.2) | copy-start | bytes 1572868
  341.8 8.4 %collective-permute-start.9 = (bf16[512,384]{0,1:T(8,128)(2,1)}, bf16[512,384]{0,1:T(8,128)(2,1)S(1)}, u32[]{:S(2)}, u32[]{:S(2)}) collective-permute-start(bf16[512,384]{0,1:T(8,128)(2,1)} %collective-permute-done.7), channel_id=1, source_target_pairs={{0,15},{1,0},{2,1},{3,2},{4,3},{5,4},{6,5},{7,6},{8,7},{9,8},{10,9... | collective-permute-start | bytes 1179656 | tf_op jit(solution)/shard_map/ppermute | solution.py:54
  344.7 11.7 %collective-permute-start.10 = (bf16[512,384]{0,1:T(8,128)(2,1)}, bf16[512,384]{0,1:T(8,128)(2,1)S(1)}, u32[]{:S(2)}, u32[]{:S(2)}) collective-permute-start(bf16[512,384]{0,1:T(8,128)(2,1)} %collective-permute-done.8), channel_id=1, source_target_pairs={{0,1},{1,2},{2,3},{3,4},{4,5},{5,6},{6,7},{7,8},{8,9},{9,10},{10,1... | collective-permute-start | bytes 1179656 | tf_op jit(solution)/shard_map/ppermute | solution.py:51
  348.2 29.4 %slice-start.1 = ((s8[6291456]{0:T(1024)(128)(4,1)}), s8[4194304]{0:T(1024)(128)(4,1)S(1)}, s32[]{:S(2)}) async-start(s8[6291456]{0:T(1024)(128)(4,1)} %bitcast.25), calls=%async_computation.5 | async-start | bytes 8388608
  350.2 11.6 %collective-permute-start.11 = (bf16[512,384]{0,1:T(8,128)(2,1)S(1)}, bf16[512,384]{0,1:T(8,128)(2,1)S(1)}, u32[]{:S(2)}, u32[]{:S(2)}) collective-permute-start(bf16[512,384]{0,1:T(8,128)(2,1)S(1)} %collective-permute-done.9), channel_id=1, source_target_pairs={{0,15},{1,0},{2,1},{3,2},{4,3},{5,4},{6,5},{7,6},{8,7},{9,8},{10,9... | collective-permute-start | bytes 1179656 | tf_op jit(solution)/shard_map/ppermute | solution.py:54
  356.4 10.6 %collective-permute-start.12 = (bf16[512,384]{0,1:T(8,128)(2,1)S(1)}, bf16[512,384]{0,1:T(8,128)(2,1)S(1)}, u32[]{:S(2)}, u32[]{:S(2)}) collective-permute-start(bf16[512,384]{0,1:T(8,128)(2,1)S(1)} %collective-permute-done.10), channel_id=1, source_target_pairs={{0,1},{1,2},{2,3},{3,4},{4,5},{5,6},{6,7},{7,8},{8,9},{9,10},{10,1... | collective-permute-start | bytes 1179656 | tf_op jit(solution)/shard_map/ppermute | solution.py:51
  361.7 9.7 %collective-permute-start.13 = (bf16[512,384]{0,1:T(8,128)(2,1)S(1)}, bf16[512,384]{0,1:T(8,128)(2,1)S(1)}, u32[]{:S(2)}, u32[]{:S(2)}) collective-permute-start(bf16[512,384]{0,1:T(8,128)(2,1)S(1)} %collective-permute-done.11), channel_id=1, source_target_pairs={{0,15},{1,0},{2,1},{3,2},{4,3},{5,4},{6,5},{7,6},{8,7},{9,8},{10,9... | collective-permute-start | bytes 1179656 | tf_op jit(solution)/shard_map/ppermute | solution.py:54
  367.0 9.9 %collective-permute-start.14 = (bf16[512,384]{0,1:T(8,128)(2,1)S(1)}, bf16[512,384]{0,1:T(8,128)(2,1)S(1)}, u32[]{:S(2)}, u32[]{:S(2)}) collective-permute-start(bf16[512,384]{0,1:T(8,128)(2,1)S(1)} %collective-permute-done.12), channel_id=1, source_target_pairs={{0,1},{1,2},{2,3},{3,4},{4,5},{5,6},{6,7},{7,8},{8,9},{9,10},{10,1... | collective-permute-start | bytes 1179656 | tf_op jit(solution)/shard_map/ppermute | solution.py:51
  377.6 8.1 %copy-start.2 = (f32[512,512]{1,0:T(8,128)S(1)}, f32[512,512]{1,0:T(8,128)}, u32[]{:S(2)}) copy-start(f32[512,512]{1,0:T(8,128)} %all-reduce.2.cloned.1.call-done) | copy-start | bytes 3145732
Sparse Core Ops, SparseCore 0:
  23.1 137.3 reduce-scatter.1
  162.6 74.4 all-gather.1
  240.5 93.7 all-reduce.1
